TPU v7x, 256 devices: a whole 4x4x8 slice. The times are simulated.
256 devices in a mesh: gx: 8 (over x, core), gy: 32 (over y, z).
Axes of the slice: x: 4, y: 4, z: 8, core: 2. Of those that a mesh axis runs over, the one named last changes fastest.
Arguments:
- hidden_in: bfloat16 [8192, 4096], P('gx', 'gy')
- norm_gain: bfloat16 [4096], P('gy'), may hold values from 0.099609375 to 1.8984375
- query_proj: bfloat16 [4096, 4096], P('gx', 'gy')
- kv_proj: bfloat16 [1024, 4096], P(None, 'gy')
- prompt_lengths: int32 [8], replicated, may hold values from 1 to 4096, 8192 in all
- cache_slot: int32 [512], replicated, may hold values from 0 to 511, as said below
Outputs:
- attention: bfloat16 [8192, 4096], P('gy', 'gx')
- kv_cache: bfloat16 [512, 16, 1024], P('gy', None, 'gx')
Inputs may be any that keep to these rules, and one draw needn't show every extreme that they name: `prompt_lengths`: the 8 prompts sum to 8192 tokens; the longest has exactly 4096. `cache_slot`: A permutation of the 512 slots; slot s is held by index s // 16 of gy. The 16 pages of one token block go to any one index at most 1 times, and every index receives exactly 16 pages.
All inputs are finite; a program needn't handle non-finite values.
Results may differ from a plain program's by a relative error of at most 0.0066.
The roundings to bfloat16 on the way count: a program that leaves them out, or rounds other values in their place, can miss the bound.
Values may be sent and summed in bfloat16 or wider, within the bound.
No kernel may reach another device: no remote copies, remote signals or barrier semaphores. Data moves between devices by JAX's collectives and lax.ppermute only.
A program may use at most 128 MiB of HBM per device.

v0:
```python
import math
import jax
import jax.numpy as jnp
from jax import lax
from jax.sharding import PartitionSpec as P

D = 4096
H = 32
KVH = 4
HD = 128
PAGES_DEV = 16
MOST = 4096
epsilon = 1e-06
rope_base = 5000000.0
masked_out = -1e30


def token_places(prompt_lengths, token_index):
    prompt_ends = jnp.cumsum(prompt_lengths)
    prompt_starts = prompt_ends - prompt_lengths
    segment = jnp.sum((token_index[:, None] >= prompt_ends[None, :]).astype(jnp.int32), axis=1)
    chosen = segment[:, None] == jnp.arange(prompt_lengths.shape[0], dtype=jnp.int32)[None, :]
    opening = jnp.sum(jnp.where(chosen, prompt_starts[None, :], 0), axis=1)
    return (segment, token_index - opening)


def rotate(vectors, places):
    half_size = vectors.shape[-1] // 2
    frequency = rope_base ** (-(jnp.arange(half_size, dtype=jnp.float32) * 2.0) / vectors.shape[-1])
    angles = places.astype(jnp.float32)[:, None] * frequency[None, :]
    cos_part = jnp.cos(angles)[:, None, :]
    sin_part = jnp.sin(angles)[:, None, :]
    leading = vectors[..., :half_size]
    trailing = vectors[..., half_size:]
    return jnp.concatenate(
        [leading * cos_part - trailing * sin_part, trailing * cos_part + leading * sin_part],
        axis=-1,
    )


def local(hidden_in, norm_gain, query_proj, kv_proj, prompt_lengths, cache_slot):
    count_gx = lax.axis_size("gx")
    count_gy = lax.axis_size("gy")
    where_gx = lax.axis_index("gx")
    where_gy = lax.axis_index("gy")
    local_rows, local_feats = hidden_in.shape
    features = local_feats * count_gy
    block_tokens = local_rows * count_gx // count_gy
    all_tokens = block_tokens * count_gy
    blocks_per_slab = local_rows // block_tokens
    sub = block_tokens // count_gy
    heads_here = query_proj.shape[0] // HD
    query_cols = heads_here * HD
    is_key = where_gx % 2 == 0
    kv_rows = lax.dynamic_slice_in_dim(kv_proj, where_gx * HD, HD, 0)
    gain_rows = jnp.concatenate(
        [norm_gain[None, :], jnp.zeros((7, local_feats), norm_gain.dtype)], axis=0
    )
    stacked = jnp.concatenate([query_proj, kv_rows, gain_rows], axis=0)
    gathered = lax.all_gather(stacked, "gy", axis=1, tiled=True)
    weight_rows = query_cols + HD
    weights_full = gathered[:weight_rows]
    gain_full = gathered[weight_rows]
    pieces = hidden_in.reshape(blocks_per_slab, count_gy, sub, local_feats)
    pieces = lax.all_to_all(pieces, "gy", 1, 1, tiled=True)
    spread = jnp.broadcast_to(pieces[None], (count_gx,) + pieces.shape)
    rows_here = lax.all_to_all(spread, "gx", 0, 0, tiled=True)
    rows_here = rows_here.transpose(0, 1, 3, 2, 4).reshape(block_tokens, features)
    widened = rows_here.astype(jnp.float32)
    squares = jnp.sum(widened * widened, axis=1)
    normed = (
        widened
        * lax.rsqrt(squares / features + epsilon)[:, None]
        * gain_full.astype(jnp.float32)[None, :]
    ).astype(jnp.bfloat16)
    contract = (((1,), (1,)), ((), ()))
    projected = lax.dot_general(normed, weights_full, contract, preferred_element_type=jnp.float32)
    order = jnp.arange(block_tokens, dtype=jnp.int32)
    my_tokens = order // sub * block_tokens + where_gy * sub + order % sub
    unused_segment, my_places = token_places(prompt_lengths, my_tokens)
    queries = rotate(
        projected[:, :query_cols].reshape(block_tokens, heads_here, HD), my_places
    ).astype(jnp.bfloat16)
    half_raw = projected[:, query_cols:]
    rotated = rotate(half_raw[:, None, :], my_places)[:, 0, :]
    mine = jnp.where(is_key, rotated, half_raw).astype(jnp.bfloat16)
    window_blocks = min(count_gy, MOST // block_tokens + 1)
    window = window_blocks * block_tokens
    first_blocks = [
        min(max(b - (window_blocks - 1), 0), count_gy - window_blocks) for b in range(count_gy)
    ]
    chosen = jnp.asarray(
        [[f + w for w in range(window_blocks)] for f in first_blocks], dtype=jnp.int32
    )
    strided = mine.reshape(count_gy, sub, HD)
    kv_parcel = jnp.take(strided, chosen, axis=0).reshape(count_gy, window_blocks * sub * HD)
    q_parcel = queries.reshape(count_gy, sub * query_cols)
    parcel = jnp.concatenate([q_parcel, kv_parcel], axis=1)
    arrived = lax.all_to_all(parcel, "gy", 0, 0, tiled=True)
    queries = arrived[:, : sub * query_cols].reshape(block_tokens, heads_here, HD)
    mine_window = arrived[:, sub * query_cols :].reshape(count_gy, window_blocks, sub, HD)
    other_window = lax.ppermute(mine_window, "gx", [(p, p ^ 1) for p in range(count_gx)])
    key_rows = jnp.where(is_key, mine_window, other_window).reshape(window, HD)
    value_rows = jnp.where(is_key, other_window, mine_window).reshape(window, HD)
    first_query = where_gy * block_tokens
    token_index = first_query + order
    segment_own, unused_places = token_places(prompt_lengths, token_index)
    window_first = jnp.clip(where_gy - (window_blocks - 1), 0, count_gy - window_blocks)
    source_range = jnp.arange(count_gy, dtype=jnp.int32)[:, None, None]
    block_range = jnp.arange(window_blocks, dtype=jnp.int32)[None, :, None]
    sub_range = jnp.arange(sub, dtype=jnp.int32)[None, None, :]
    key_index = (
        (window_first + block_range) * block_tokens + source_range * sub + sub_range
    ).reshape(window)
    key_segment, unused_places = token_places(prompt_lengths, key_index)
    allowed = (key_segment[None, :] == segment_own[:, None]) & (
        key_index[None, :] <= token_index[:, None]
    )
    score_scale = 1.0 / math.sqrt(HD)
    scores = (
        jnp.einsum("qhd,kd->hqk", queries, key_rows, preferred_element_type=jnp.float32)
        * score_scale
    )
    scores = jnp.where(allowed[None], scores, masked_out)
    row_max = jnp.max(scores, axis=2, keepdims=True)
    weights = jnp.where(allowed[None], jnp.exp(scores - row_max), 0.0)
    totals = jnp.sum(weights, axis=2)
    mixed = jnp.einsum(
        "hqk,kd->hqd", weights.astype(jnp.bfloat16), value_rows, preferred_element_type=jnp.float32
    )
    attention = (
        (mixed / totals[..., None])
        .astype(jnp.bfloat16)
        .transpose(1, 0, 2)
        .reshape(block_tokens, query_cols)
    )
    cache_cols = lax.dynamic_index_in_dim(
        mine_window, where_gy - window_first, 1, keepdims=False
    ).reshape(block_tokens, HD)
    pages_dev = PAGES_DEV
    page_len = block_tokens // pages_dev
    page_range = jnp.arange(pages_dev, dtype=jnp.int32)
    width_cols = cache_cols.shape[1]
    my_pages = cache_cols.reshape(pages_dev, page_len * width_cols)
    capacity = max(1, pages_dev // count_gy)
    slots_all = count_gy * capacity
    owners = (cache_slot // pages_dev).reshape(count_gy, pages_dev)
    earlier = page_range[None, :] < page_range[:, None]
    same_owner = owners[:, :, None] == owners[:, None, :]
    ranks = jnp.sum((same_owner & earlier[None]).astype(jnp.int32), axis=2)
    my_owner = lax.dynamic_index_in_dim(owners, where_gy, 0, keepdims=False)
    my_rank = lax.dynamic_index_in_dim(ranks, where_gy, 0, keepdims=False)
    target = my_owner * capacity + my_rank
    slot_range = jnp.arange(slots_all, dtype=jnp.int32)
    send_map = (slot_range[:, None] == target[None, :]).astype(jnp.bfloat16)
    outgoing = jnp.dot(send_map, my_pages, preferred_element_type=jnp.float32).astype(jnp.bfloat16)
    incoming = lax.all_to_all(outgoing, "gy", split_axis=0, concat_axis=0, tiled=True)
    wanted = where_gy * pages_dev + page_range
    matches = cache_slot[None, :] == wanted[:, None]
    page_ids = jnp.arange(cache_slot.shape[0], dtype=jnp.int32)
    source_page = jnp.sum(jnp.where(matches, page_ids[None, :], 0), axis=1)
    source_rank = jnp.sum(jnp.where(matches, ranks.reshape(-1)[None, :], 0), axis=1)
    source_slot = source_page // pages_dev * capacity + source_rank
    take_map = (source_slot[:, None] == slot_range[None, :]).astype(jnp.bfloat16)
    cache_block = jnp.dot(take_map, incoming, preferred_element_type=jnp.float32)
    cache_block = cache_block.astype(jnp.bfloat16).reshape(pages_dev, page_len, width_cols)
    return (attention, cache_block)


def solution(mesh):
    return jax.shard_map(
        local,
        mesh=mesh,
        in_specs=(P("gx", "gy"), P("gy"), P("gx", "gy"), P(None, "gy"), P(), P()),
        out_specs=(P("gy", "gx"), P("gy", None, "gx")),
        check_vma=False,
    )
```

profile of v0, /device:TPU:2, one launch (start us, length us, event | category | flops | bytes accessed | tf_op | source)
XLA Modules:
  0.0 227.4 jit_solution(1769382629200644866)
XLA Ops:
  8.1 1.7 maximum_maximum_fusion
  9.9 1.0 copy.42
  10.9 23.8 %all_to_all.34 = bf16[4,32,8,128]{3,2,0,1:T(8,128)(2,1)S(1)} all-to-all(bf16[4,32,8,128]{3,2,0,1:T(8,128)(2,1)S(1)} %copy.42), channel_id=1, replica_groups=mesh['gx'=8,'gy'=32] {'gy'}, dimensions={1} | all-to-all | bytes 524288 | tf_op jit(solution)/shard_map/all_to_all | solution.py:65
  34.8 1.8 broadcast_in_dim.67
  36.6 4.7 %all-to-all-start.1 = ((bf16[8,4,32,8,128]{4,3,2,1,0:T(8,128)(2,1)}), bf16[8,4,32,8,128]{4,3,2,1,0:T(8,128)(2,1)S(1)}, u32[]{:S(2)}, u32[]{:S(2)}) async-start(bf16[8,4,32,8,128]{4,3,2,1,0:T(8,128)(2,1)} %broadcast_in_dim.67), calls=%async_computation.1 | async-start | bytes 4194304 | tf_op jit(solution)/shard_map/all_to_all | solution.py:67
  42.3 24.8 %all-to-all-done.1 = bf16[8,4,32,8,128]{4,3,2,1,0:T(8,128)(2,1)S(1)} async-done(((bf16[8,4,32,8,128]{4,3,2,1,0:T(8,128)(2,1)}), bf16[8,4,32,8,128]{4,3,2,1,0:T(8,128)(2,1)S(1)}, u32[]{:S(2)}, u32[]{:S(2)}) %all-to-all-start.1) | async-done | bytes 2097184 | tf_op jit(solution)/shard_map/all_to_all | solution.py:67
  67.7 2.5 %convert_element_type.78 = f32[8,4,32,8,128]{4,3,2,1,0:T(8,128)} convert(bf16[8,4,32,8,128]{4,3,2,1,0:T(8,128)(2,1)S(1)} %all-to-all-done.1) | non-fusion elementwise | flops 1048576 | bytes 6291456 | tf_op jit(solution)/shard_map/convert_element_type | solution.py:69
  70.2 31.7 %all-gather.2.cloned.1.call-done = bf16[648,4096]{1,0:T(8,128)(2,1)} async-done(((bf16[648,128]{1,0:T(8,128)(2,1)}), bf16[648,4096]{1,0:T(8,128)(2,1)}) %all-gather.2.cloned.1.call-update) | async-done | bytes 5308432 | tf_op jit(solution)/shard_map/all_gather | solution.py:60
  102.8 5.6 %fusion.7 = f32[256,640]{1,0:T(8,128)S(1)} fusion(bf16[648,4096]{1,0:T(8,128)(2,1)} %all-gather.2.cloned.1.call-done, f32[256,4096]{1,0:T(8,128)} %bitcast.75, f32[4096]{0:T(1024)S(1)} %bitcast.80, f32[256]{0:T(256)S(1)} %rsqrt.11), kind=kOutput, calls=%fused_computation.10 | convolution fusion | flops 1345323008 | bytes 10109952 | tf_op jit(solution)/shard_map/dot_general | solution.py:77
  110.4 2.5 %gather_fusion = bf16[544,8,128]{2,1,0:T(8,128)(2,1)S(1)} fusion(bf16[32,8,128]{2,1,0:T(8,128)(2,1)S(1)} %fusion.34, s32[1024]{0:T(1024)S(1)} %pad_clamp_fusion), kind=kCustom, calls=%fused_computation | custom fusion | bytes 2230400 | tf_op jit(solution)/shard_map/jit(_take)/gather | solution.py:96
  114.0 1.7 reduce.4
  115.7 1.9 reshape.420
  117.6 9.7 %all-to-all-start.2 = ((bf16[32,2,10752]{2,1,0:T(2,128)(2,1)}), bf16[32,2,10752]{2,1,0:T(2,128)(2,1)}, u32[]{:S(2)}, u32[]{:S(2)}) async-start(bf16[32,2,10752]{2,1,0:T(2,128)(2,1)} %reshape.420), calls=%async_computation.2 | async-start | bytes 2752512 | tf_op jit(solution)/shard_map/all_to_all | solution.py:99
  127.8 4.4 %compare_and_fusion = pred[256,4352]{0,1:T(8,128)(4,1)} fusion(s32[256]{0:T(256)S(1)} %get-tuple-element.29, s32[256]{0:T(256)S(1)} %get-tuple-element.16, s32[4352]{0:T(1024)S(1)} %add.184, s32[4352]{0:T(1024)S(1)} %convert_reduce_fusion), kind=kLoop, calls=%fused_computation.12 | loop fusion | flops 3342336 | bytes 1150976 | tf_op jit(solution)/shard_map/and | solution.py:116
  132.2 25.2 %all-to-all-done.2 = bf16[32,2,10752]{2,1,0:T(2,128)(2,1)} async-done(((bf16[32,2,10752]{2,1,0:T(2,128)(2,1)}), bf16[32,2,10752]{2,1,0:T(2,128)(2,1)}, u32[]{:S(2)}, u32[]{:S(2)}) %all-to-all-start.2) | async-done | bytes 1376288 | tf_op jit(solution)/shard_map/all_to_all | solution.py:99
  157.4 7.8 %reshape.421 = bf16[32,1,21504]{2,1,0:T(2,128)(2,1)S(1)} reshape(bf16[32,2,10752]{2,1,0:T(2,128)(2,1)} %all-to-all-done.2) | data formatting | bytes 2752512
  165.7 1.1 copy-done.1
  169.6 5.4 %all-to-all-start.3 = ((bf16[32,2,1024]{2,1,0:T(2,128)(2,1)}), bf16[32,2,1024]{2,1,0:T(2,128)(2,1)S(1)}, u32[]{:S(2)}, u32[]{:S(2)}) async-start(bf16[32,2,1024]{2,1,0:T(2,128)(2,1)} %reshape.422), calls=%async_computation.3 | async-start | bytes 262144 | tf_op jit(solution)/shard_map/all_to_all | solution.py:157
  175.2 1.0 slice.51
  176.4 9.6 %all-to-all-done.3 = bf16[32,2,1024]{2,1,0:T(2,128)(2,1)S(1)} async-done(((bf16[32,2,1024]{2,1,0:T(2,128)(2,1)}), bf16[32,2,1024]{2,1,0:T(2,128)(2,1)S(1)}, u32[]{:S(2)}, u32[]{:S(2)}) %all-to-all-start.3) | async-done | bytes 131104 | tf_op jit(solution)/shard_map/all_to_all | solution.py:157
  186.9 1.2 broadcast_select_fusion.1
  188.1 8.6 %fusion.22 = f32[4352,256,4]{1,0,2:T(8,128)} fusion(bf16[4352,128,1]{1,0,2:T(8,128)(2,1)S(1)} %bitcast.74, bf16[256,4,128]{2,1,0:T(4,128)(2,1)S(1)} %reshape.401), kind=kOutput, calls=%fused_computation.33 | convolution fusion | flops 1140850688 | bytes 19202048 | tf_op jit(solution)/shard_map/qhd,kd->hqk/dot_general | solution.py:121
  196.7 18.1 %fusion.49 = (f32[4,256]{1,0:T(4,128)S(1)}, bf16[4,256,4352]{1,2,0:T(8,128)(2,1)}) fusion(f32[4352,256,4]{1,0,2:T(8,128)} %fusion.22, pred[256,4352]{0,1:T(8,128)(4,1)S(1)} %copy-done.2), kind=kOutput, calls=%fused_computation.106 | output fusion | flops 35655936 | bytes 27856896 | tf_op jit(solution)/shard_map/sub | solution.py:126
  214.8 5.0 %fusion.18 = bf16[256,4,128]{0,2,1:T(8,128)(2,1)S(1)} fusion(bf16[4352,128,1]{1,0,2:T(8,128)(2,1)S(1)} %bitcast.76, bf16[4,256,4352]{1,2,0:T(8,128)(2,1)} %get-tuple-element.27, f32[256,4]{0,1:T(4,128)S(1)} %bitcast.85), kind=kOutput, calls=%fused_computation.24 | convolution fusion | flops 1141112832 | bytes 10293248 | tf_op jit(solution)/shard_map/hqk,kd->hqd/dot_general | solution.py:128
  (75 shorter events, 12.3 us)
Async XLA Ops:
  7.2 1.0 copy-start
  7.2 94.8 %all-gather.2.cloned.1.call-start = ((), (), s32[]{:S(2)}) async-start(), calls=%async_computation.4 | async-start | bytes 5474304 | tf_op jit(solution)/shard_map/all_gather | solution.py:60
  34.8 6.6 %copy-start.6 = (s32[8]{0:T(128)S(1)}, s32[8]{0:T(128)}, u32[]{:S(2)}) copy-start(s32[8]{0:T(128)} %param.11) | copy-start | bytes 100
  34.8 6.8 %copy-start.5 = (s32[544]{0:T(1024)S(1)}, s32[544]{0:T(1024)}, u32[]{:S(2)}) copy-start(s32[544]{0:T(1024)} %constant.153) | copy-start | bytes 6532
  36.6 30.5 %all-to-all-start.1 = ((bf16[8,4,32,8,128]{4,3,2,1,0:T(8,128)(2,1)}), bf16[8,4,32,8,128]{4,3,2,1,0:T(8,128)(2,1)S(1)}, u32[]{:S(2)}, u32[]{:S(2)}) async-start(bf16[8,4,32,8,128]{4,3,2,1,0:T(8,128)(2,1)} %broadcast_in_dim.67), calls=%async_computation.1 | async-start | bytes 4194304 | tf_op jit(solution)/shard_map/all_to_all | solution.py:67
  117.6 39.8 %all-to-all-start.2 = ((bf16[32,2,10752]{2,1,0:T(2,128)(2,1)}), bf16[32,2,10752]{2,1,0:T(2,128)(2,1)}, u32[]{:S(2)}, u32[]{:S(2)}) async-start(bf16[32,2,10752]{2,1,0:T(2,128)(2,1)} %reshape.420), calls=%async_computation.2 | async-start | bytes 2752512 | tf_op jit(solution)/shard_map/all_to_all | solution.py:99
  165.7 1.1 copy-start.1
  165.7 1.6 copy-start.4
  167.0 19.9 %collective-permute-start = (bf16[32,17,8,128]{3,2,1,0:T(8,128)(2,1)S(1)}, bf16[32,17,8,128]{3,2,1,0:T(8,128)(2,1)S(1)}, u32[]{:S(2)}, u32[]{:S(2)}) collective-permute-start(bf16[32,17,8,128]{3,2,1,0:T(8,128)(2,1)S(1)} %bitcast.71), channel_id=1, source_target_pairs={{0,32},{32,0},{64,96},{96,64},{128,160},{160,128},{192,224},{224,1... | collective-permute-start | bytes 3342344 | tf_op jit(solution)/shard_map/ppermute | solution.py:102
  169.6 16.3 %all-to-all-start.3 = ((bf16[32,2,1024]{2,1,0:T(2,128)(2,1)}), bf16[32,2,1024]{2,1,0:T(2,128)(2,1)S(1)}, u32[]{:S(2)}, u32[]{:S(2)}) async-start(bf16[32,2,1024]{2,1,0:T(2,128)(2,1)} %reshape.422), calls=%async_computation.3 | async-start | bytes 262144 | tf_op jit(solution)/shard_map/all_to_all | solution.py:157
  188.1 8.6 %copy-start.2 = (pred[256,4352]{0,1:T(8,128)(4,1)S(1)}, pred[256,4352]{0,1:T(8,128)(4,1)}, u32[]{:S(2)}) copy-start(pred[256,4352]{0,1:T(8,128)(4,1)} %compare_and_fusion) | copy-start | bytes 3342340
  196.7 18.1 %copy-start.3 = (bf16[32,17,8,128]{3,2,1,0:T(8,128)(2,1)S(1)}, bf16[32,17,8,128]{3,2,1,0:T(8,128)(2,1)}, u32[]{:S(2)}) copy-start(bf16[32,17,8,128]{3,2,1,0:T(8,128)(2,1)} %get-tuple-element.19) | copy-start | bytes 3342340
Sparse Core Ops, SparseCore 0:
  11.0 90.8 all-gather.1
where the time goes:
time: 228 us; the launch traced here: 227 us
  waiting for transfers between devices  91.3 us (40%)
  other arithmetic  35 us (15%)
  blocking collectives  23.8 us (10%)
  local copies, waits for them, and re-layouts  23.2 us (10%)
  starting transfers between devices  20.1 us (9%)
  matrix products  19.5 us (9%)
  between operations  14.4 us (6%)
    all_gather x1, waiting for transfers between devices, local(): gathered = lax.all_gather(stacked, 'gy', axis=1, tiled=True)  31.7 us
    all_to_all x1, waiting for transfers between devices, local(): arrived = lax.all_to_all(parcel, 'gy', 0, 0, tiled=True)  25.2 us
    all_to_all x1, waiting for transfers between devices, local(): rows_here = lax.all_to_all(spread, 'gx', 0, 0, tiled=True)  24.8 us
    all_to_all x1, blocking collectives, local(): pieces = lax.all_to_all(pieces, 'gy', 1, 1, tiled=True)  23.8 us
    sub x1, other arithmetic, local(): weights = jnp.where(allowed[None], jnp.exp(scores - row_max), 0.0)  18.1 us
    unnamed x23, local copies, waits for them, and re-layouts  14.6 us
    all_to_all x1, starting transfers between devices, local(): arrived = lax.all_to_all(parcel, 'gy', 0, 0, tiled=True)  9.68 us
    all_to_all x1, waiting for transfers between devices, local(): lax.all_to_all(outgoing, 'gy', split_axis=0, concat_axis=0, tiled=True)  9.57 us
  transfers between devices with their start and end apart: 5, of which 4 were waited for; matrix products, arithmetic and copies ran while one was open for 7% of the time, Pallas kernels for 0%

commit v1 on v0

--- a/solution.py
+++ b/solution.py
@@ -57,7 +57,15 @@
         [norm_gain[None, :], jnp.zeros((7, local_feats), norm_gain.dtype)], axis=0
     )
     stacked = jnp.concatenate([query_proj, kv_rows, gain_rows], axis=0)
-    gathered = lax.all_gather(stacked, "gy", axis=1, tiled=True)
+    gathered = jnp.concatenate(
+        lax.all_to_all(
+            jnp.stack(lax.axis_size("gy") * [stacked], 0),
+            axis_name="gy",
+            concat_axis=0,
+            split_axis=0,
+        ),
+        1,
+    )
     weight_rows = query_cols + HD
     weights_full = gathered[:weight_rows]
     gain_full = gathered[weight_rows]

time: 228 us -> 322 us (1.41)
  waiting for transfers between devices: 91.3 us -> 182 us
  local copies, waits for them, and re-layouts: 23.2 us -> 40.9 us
  between operations: 14.4 us -> 1.06 us
  other arithmetic: 35 us -> 30.8 us
  starting transfers between devices: 20.1 us -> 23.8 us
    all_to_all x0 -> x1, waiting for transfers between devices: none -> 117 us  [local(): lax.all_to_all(jnp.stack(lax.axis_size('gy') * [stacked], 0), axis_name='...]
    all_gather x1 -> x0, waiting for transfers between devices: 31.7 us -> none  [local(): gathered = lax.all_gather(stacked, 'gy', axis=1, tiled=True)]
    slice x0 -> x2, local copies, waits for them, and re-layouts: none -> 12.1 us  [local(): weights_full = gathered[:weight_rows]]
    all_to_all x0 -> x1, starting transfers between devices: none -> 5.18 us  [local(): lax.all_to_all(jnp.stack(lax.axis_size('gy') * [stacked], 0), axis_name='...]
    all_to_all x1, waiting for transfers between devices: 25.2 us -> 30.4 us  [local(): arrived = lax.all_to_all(parcel, 'gy', 0, 0, tiled=True)]
    all_to_all x0 -> x1, local copies, waits for them, and re-layouts: none -> 3.35 us  [local(): lax.all_to_all(jnp.stack(lax.axis_size('gy') * [stacked], 0), axis_name='...]
    unnamed x23 -> x29, local copies, waits for them, and re-layouts: 14.6 us -> 13.8 us
  transfers between devices with their start and end apart: 5 -> 5, of which waited for: 4 -> 4; matrix products, arithmetic and copies ran while one was open for 7% -> 3% of each run, Pallas kernels for 0% -> 0%
where the time goes in v1:
time: 322 us; the launch traced here: 321 us
  waiting for transfers between devices  182 us (57%)
  local copies, waits for them, and re-layouts  40.9 us (13%)
  other arithmetic  30.8 us (10%)
  starting transfers between devices  23.8 us (7%)
  blocking collectives  23.7 us (7%)
  matrix products  18.3 us (6%)
    all_to_all x1, waiting for transfers between devices, local(): lax.all_to_all(jnp.stack(lax.axis_size('gy') * [stacked], 0), axis_name='...  117 us
    all_to_all x1, waiting for transfers between devices, local(): arrived = lax.all_to_all(parcel, 'gy', 0, 0, tiled=True)  30.4 us
    all_to_all x1, waiting for transfers between devices, local(): rows_here = lax.all_to_all(spread, 'gx', 0, 0, tiled=True)  25.4 us
    all_to_all x1, blocking collectives, local(): pieces = lax.all_to_all(pieces, 'gy', 1, 1, tiled=True)  23.7 us
    sub x1, other arithmetic, local(): weights = jnp.where(allowed[None], jnp.exp(scores - row_max), 0.0)  18.1 us
    unnamed x29, local copies, waits for them, and re-layouts  13.8 us
    slice x2, local copies, waits for them, and re-layouts, local(): weights_full = gathered[:weight_rows]  12.1 us
    all_to_all x1, waiting for transfers between devices, local(): lax.all_to_all(outgoing, 'gy', split_axis=0, concat_axis=0, tiled=True)  9.57 us
  transfers between devices with their start and end apart: 5, of which 4 were waited for; matrix products, arithmetic and copies ran while one was open for 3% of the time, Pallas kernels for 0%

profile of v1, /device:TPU:2, one launch (start us, length us, event | category | flops | bytes accessed | tf_op | source)
XLA Modules:
  0.0 320.9 jit_solution(5536689947217154078)
XLA Ops:
  1.7 23.7 %all_to_all.39 = bf16[4,32,8,128]{3,2,0,1:T(8,128)(2,1)S(1)} all-to-all(bf16[4,32,8,128]{3,2,0,1:T(8,128)(2,1)S(1)} %copy.55), channel_id=1, replica_groups=mesh['gx'=8,'gy'=32] {'gy'}, dimensions={1} | all-to-all | bytes 524288 | tf_op jit(solution)/shard_map/all_to_all | solution.py:73
  25.5 1.8 broadcast_in_dim.67
  27.3 4.8 %all-to-all-start.1 = ((bf16[8,4,32,8,128]{4,3,2,1,0:T(8,128)(2,1)}), bf16[8,4,32,8,128]{4,3,2,1,0:T(8,128)(2,1)S(1)}, u32[]{:S(2)}, u32[]{:S(2)}) async-start(bf16[8,4,32,8,128]{4,3,2,1,0:T(8,128)(2,1)} %broadcast_in_dim.67), calls=%async_computation.1 | async-start | bytes 4194304 | tf_op jit(solution)/shard_map/all_to_all | solution.py:75
  32.4 25.4 %all-to-all-done.1 = bf16[8,4,32,8,128]{4,3,2,1,0:T(8,128)(2,1)S(1)} async-done(((bf16[8,4,32,8,128]{4,3,2,1,0:T(8,128)(2,1)}), bf16[8,4,32,8,128]{4,3,2,1,0:T(8,128)(2,1)S(1)}, u32[]{:S(2)}, u32[]{:S(2)}) %all-to-all-start.1) | async-done | bytes 2097184 | tf_op jit(solution)/shard_map/all_to_all | solution.py:75
  57.9 3.0 stack.2
  60.9 5.2 %all-to-all-start.2 = ((bf16[32,648,128]{2,1,0:T(8,128)(2,1)}), bf16[32,648,128]{2,1,0:T(8,128)(2,1)}, u32[]{:S(2)}, u32[]{:S(2)}) async-start(bf16[32,648,128]{2,1,0:T(8,128)(2,1)} %stack.2), calls=%async_computation.2 | async-start | bytes 10616832 | tf_op jit(solution)/shard_map/all_to_all | solution.py:61
  67.6 116.9 %all-to-all-done.2 = bf16[32,648,128]{2,1,0:T(8,128)(2,1)} async-done(((bf16[32,648,128]{2,1,0:T(8,128)(2,1)}), bf16[32,648,128]{2,1,0:T(8,128)(2,1)}, u32[]{:S(2)}, u32[]{:S(2)}) %all-to-all-start.2) | async-done | bytes 5308448 | tf_op jit(solution)/shard_map/all_to_all | solution.py:61
  184.5 3.4 %copy.84 = bf16[32,648,128]{2,0,1:T(8,128)(2,1)S(1)} copy(bf16[32,648,128]{2,1,0:T(8,128)(2,1)} %all-to-all-done.2) | data formatting | bytes 10616832 | tf_op jit(solution)/shard_map/all_to_all | solution.py:61
  187.9 3.2 %slice.48 = bf16[640,32,128]{2,1,0:T(8,128)(2,1)} slice(bf16[648,32,128]{2,1,0:T(8,128)(2,1)S(1)} %bitcast.80), slice={[0:640], [0:32], [0:128]} | slice | bytes 10485760 | tf_op jit(solution)/shard_map/slice | solution.py:70
  191.1 8.9 %copy.58 = bf16[640,32,128]{0,2,1:T(8,128)(2,1)} copy(bf16[640,32,128]{2,1,0:T(8,128)(2,1)} %slice.48) | data formatting | bytes 10485760 | tf_op jit(solution)/shard_map/slice | solution.py:70
  200.7 4.3 %fusion.50 = f32[256,640]{1,0:T(8,128)S(1)} fusion(bf16[256,4096]{1,0:T(8,128)(2,1)S(1)} %bitcast.88, bf16[640,4096]{0,1:T(8,128)(2,1)} %bitcast.83), kind=kOutput, calls=%fused_computation.108 | convolution fusion | flops 1342177280 | bytes 7995392 | tf_op jit(solution)/shard_map/dot_general | solution.py:85
  207.0 2.5 gather_fusion
  210.7 1.7 reduce.4
  212.4 1.9 reshape.439
  214.3 8.3 %all-to-all-start.3 = ((bf16[32,2,10752]{2,1,0:T(2,128)(2,1)}), bf16[32,2,10752]{2,1,0:T(2,128)(2,1)}, u32[]{:S(2)}, u32[]{:S(2)}) async-start(bf16[32,2,10752]{2,1,0:T(2,128)(2,1)} %reshape.439), calls=%async_computation.3 | async-start | bytes 2752512 | tf_op jit(solution)/shard_map/all_to_all | solution.py:107
  223.1 4.4 %compare_and_fusion = pred[256,4352]{0,1:T(8,128)(4,1)} fusion(s32[256]{0:T(256)S(1)} %get-tuple-element.31, s32[256]{0:T(256)S(1)} %get-tuple-element.18, s32[4352]{0:T(1024)S(1)} %add.183, s32[4352]{0:T(1024)S(1)} %convert_reduce_fusion), kind=kLoop, calls=%fused_computation.13 | loop fusion | flops 3342336 | bytes 1150976 | tf_op jit(solution)/shard_map/and | solution.py:124
  227.5 30.4 %all-to-all-done.3 = bf16[32,2,10752]{2,1,0:T(2,128)(2,1)} async-done(((bf16[32,2,10752]{2,1,0:T(2,128)(2,1)}), bf16[32,2,10752]{2,1,0:T(2,128)(2,1)}, u32[]{:S(2)}, u32[]{:S(2)}) %all-to-all-start.3) | async-done | bytes 1376288 | tf_op jit(solution)/shard_map/all_to_all | solution.py:107
  257.8 7.8 %reshape.440 = bf16[32,1,21504]{2,1,0:T(2,128)(2,1)S(1)} reshape(bf16[32,2,10752]{2,1,0:T(2,128)(2,1)} %all-to-all-done.3) | data formatting | bytes 2752512
  269.9 5.4 %all-to-all-start.4 = ((bf16[32,2,1024]{2,1,0:T(2,128)(2,1)}), bf16[32,2,1024]{2,1,0:T(2,128)(2,1)S(1)}, u32[]{:S(2)}, u32[]{:S(2)}) async-start(bf16[32,2,1024]{2,1,0:T(2,128)(2,1)} %reshape.441), calls=%async_computation.4 | async-start | bytes 262144 | tf_op jit(solution)/shard_map/all_to_all | solution.py:165
  276.6 9.6 %all-to-all-done.4 = bf16[32,2,1024]{2,1,0:T(2,128)(2,1)S(1)} async-done(((bf16[32,2,1024]{2,1,0:T(2,128)(2,1)}), bf16[32,2,1024]{2,1,0:T(2,128)(2,1)S(1)}, u32[]{:S(2)}, u32[]{:S(2)}) %all-to-all-start.4) | async-done | bytes 131104 | tf_op jit(solution)/shard_map/all_to_all | solution.py:165
  287.1 1.2 broadcast_select_fusion.1
  288.3 8.6 %fusion.21 = f32[4352,256,4]{1,0,2:T(8,128)} fusion(bf16[4352,128,1]{1,0,2:T(8,128)(2,1)S(1)} %bitcast.87, bf16[256,4,128]{2,1,0:T(4,128)(2,1)S(1)} %reshape.421), kind=kOutput, calls=%fused_computation.33 | convolution fusion | flops 1140850688 | bytes 19202048 | tf_op jit(solution)/shard_map/qhd,kd->hqk/dot_general | solution.py:129
  296.9 18.1 %fusion.49 = (f32[4,256]{1,0:T(4,128)S(1)}, bf16[4,256,4352]{1,2,0:T(8,128)(2,1)}) fusion(f32[4352,256,4]{1,0,2:T(8,128)} %fusion.21, pred[256,4352]{0,1:T(8,128)(4,1)S(1)} %copy-done.3), kind=kOutput, calls=%fused_computation.107 | output fusion | flops 35655936 | bytes 27856896 | tf_op jit(solution)/shard_map/sub | solution.py:134
  315.0 5.0 %fusion.17 = bf16[256,4,128]{0,2,1:T(8,128)(2,1)S(1)} fusion(bf16[4352,128,1]{1,0,2:T(8,128)(2,1)S(1)} %bitcast.89, bf16[4,256,4352]{1,2,0:T(8,128)(2,1)} %get-tuple-element.29, f32[256,4]{0,1:T(4,128)S(1)} %bitcast.97), kind=kOutput, calls=%fused_computation.24 | convolution fusion | flops 1141112832 | bytes 10293248 | tf_op jit(solution)/shard_map/hqk,kd->hqd/dot_general | solution.py:136
  (83 shorter events, 14.3 us)
Async XLA Ops:
  0.6 31.6 %copy-start = (bf16[1024,128]{1,0:T(8,128)(2,1)S(1)}, bf16[1024,128]{1,0:T(8,128)(2,1)}, u32[]{:S(2)}) copy-start(bf16[1024,128]{1,0:T(8,128)(2,1)} %param.10) | copy-start | bytes 786436
  25.5 6.8 %copy-start.5 = (bf16[512,128]{1,0:T(8,128)(2,1)S(1)}, bf16[512,128]{1,0:T(8,128)(2,1)}, u32[]{:S(2)}) copy-start(bf16[512,128]{1,0:T(8,128)(2,1)} %param.9) | copy-start | bytes 393220
  25.5 6.8 %copy-start.8 = (bf16[128]{0:T(256)(128)(2,1)S(1)}, bf16[128]{0:T(256)(128)(2,1)}, u32[]{:S(2)}) copy-start(bf16[128]{0:T(256)(128)(2,1)} %param.8) | copy-start | bytes 772
  27.3 30.5 %all-to-all-start.1 = ((bf16[8,4,32,8,128]{4,3,2,1,0:T(8,128)(2,1)}), bf16[8,4,32,8,128]{4,3,2,1,0:T(8,128)(2,1)S(1)}, u32[]{:S(2)}, u32[]{:S(2)}) async-start(bf16[8,4,32,8,128]{4,3,2,1,0:T(8,128)(2,1)} %broadcast_in_dim.67), calls=%async_computation.1 | async-start | bytes 4194304 | tf_op jit(solution)/shard_map/all_to_all | solution.py:75
  60.9 5.2 %copy-start.9 = (s32[8]{0:T(128)S(1)}, s32[8]{0:T(128)}, u32[]{:S(2)}) copy-start(s32[8]{0:T(128)} %param.11) | copy-start | bytes 100
  60.9 5.4 %copy-start.7 = (s32[544]{0:T(1024)S(1)}, s32[544]{0:T(1024)}, u32[]{:S(2)}) copy-start(s32[544]{0:T(1024)} %constant.153) | copy-start | bytes 6532
  60.9 123.6 %all-to-all-start.2 = ((bf16[32,648,128]{2,1,0:T(8,128)(2,1)}), bf16[32,648,128]{2,1,0:T(8,128)(2,1)}, u32[]{:S(2)}, u32[]{:S(2)}) async-start(bf16[32,648,128]{2,1,0:T(8,128)(2,1)} %stack.2), calls=%async_computation.2 | async-start | bytes 10616832 | tf_op jit(solution)/shard_map/all_to_all | solution.py:61
  214.3 43.6 %all-to-all-start.3 = ((bf16[32,2,10752]{2,1,0:T(2,128)(2,1)}), bf16[32,2,10752]{2,1,0:T(2,128)(2,1)}, u32[]{:S(2)}, u32[]{:S(2)}) async-start(bf16[32,2,10752]{2,1,0:T(2,128)(2,1)} %reshape.439), calls=%async_computation.3 | async-start | bytes 2752512 | tf_op jit(solution)/shard_map/all_to_all | solution.py:107
  266.1 1.1 copy-start.2
  266.2 1.4 copy-start.6
  267.5 19.7 %collective-permute-start = (bf16[32,17,8,128]{3,2,1,0:T(8,128)(2,1)S(1)}, bf16[32,17,8,128]{3,2,1,0:T(8,128)(2,1)S(1)}, u32[]{:S(2)}, u32[]{:S(2)}) collective-permute-start(bf16[32,17,8,128]{3,2,1,0:T(8,128)(2,1)S(1)} %bitcast.84), channel_id=1, source_target_pairs={{0,32},{32,0},{64,96},{96,64},{128,160},{160,128},{192,224},{224,1... | collective-permute-start | bytes 3342344 | tf_op jit(solution)/shard_map/ppermute | solution.py:110
  269.9 16.3 %all-to-all-start.4 = ((bf16[32,2,1024]{2,1,0:T(2,128)(2,1)}), bf16[32,2,1024]{2,1,0:T(2,128)(2,1)S(1)}, u32[]{:S(2)}, u32[]{:S(2)}) async-start(bf16[32,2,1024]{2,1,0:T(2,128)(2,1)} %reshape.441), calls=%async_computation.4 | async-start | bytes 262144 | tf_op jit(solution)/shard_map/all_to_all | solution.py:165
  288.3 8.6 %copy-start.3 = (pred[256,4352]{0,1:T(8,128)(4,1)S(1)}, pred[256,4352]{0,1:T(8,128)(4,1)}, u32[]{:S(2)}) copy-start(pred[256,4352]{0,1:T(8,128)(4,1)} %compare_and_fusion) | copy-start | bytes 3342340
  296.9 18.1 %copy-start.4 = (bf16[32,17,8,128]{3,2,1,0:T(8,128)(2,1)S(1)}, bf16[32,17,8,128]{3,2,1,0:T(8,128)(2,1)}, u32[]{:S(2)}) copy-start(bf16[32,17,8,128]{3,2,1,0:T(8,128)(2,1)} %get-tuple-element.21) | copy-start | bytes 3342340
  315.0 5.9 %copy-start.1 = (bf16[1024,128]{1,0:T(8,128)(2,1)S(1)}, bf16[1024,128]{1,0:T(8,128)(2,1)}, u32[]{:S(2)}) copy-start(bf16[1024,128]{1,0:T(8,128)(2,1)} %param.10) | copy-start | bytes 786436
